TPU v7x, 256 devices: a whole 4x4x8 slice. The times are simulated.
256 devices in a mesh: wide: 64 (over x, z, core), narrow: 4 (over y).
Axes of the slice: x: 4, y: 4, z: 8, core: 2. Of those that a mesh axis runs over, the one named last changes fastest.
Arguments:
- attn_heads: bfloat16 [8192, 1536], P('wide', 'narrow'), may hold values from -6 to 6
- w_out: bfloat16 [1536, 1536], P('narrow'), may hold values from -0.21875 to 0.21875
- residual: bfloat16 [8192, 1536], P('wide', 'narrow'), may hold values from -6 to 6
- norm_gain: float32 [1536], replicated, may hold values from 0.1 to 1.9
- route_ids: int32 [8192, 4], P('wide'), may hold values from 0 to 31, all different within a row; in each aligned block of 128 rows (0 to 127, 128 to 255, ...) at most 32 rows name the same one
- route_weight: float32 [8192, 4], P('wide'), may hold values from 0.1 to 1
- row_order: int32 [8192], P('wide'), may hold values from 0 to 8191, as said below
- slot_expert: int32 [64], replicated, may hold values from 0 to 31, as said below
- w_in: bfloat16 [64, 2, 768, 1536], P('wide', None, 'narrow')
- w_down: bfloat16 [64, 768, 1536], P('wide', 'narrow')
Outputs:
- block_out: bfloat16 [8192, 1536], P('wide', 'narrow')
Inputs may be any that keep to these rules, and one draw needn't show every extreme that they name: `route_ids`: each row names 4 different experts; among the 128 rows of one index of wide no expert is named more than 32 times. `row_order`: A permutation of the rows; of the 128 rows of each index of wide, exactly 2 have their initial position among the rows of each index of wide. `slot_expert`: every expert is held by one or more slots; slots holding the same expert hold equal w_in and w_down.
All inputs are finite; a program needn't handle non-finite values.
Results may differ from a plain program's by a relative error of at most 0.017.
Values may be sent and summed in bfloat16 or wider, within the bound.
No kernel may reach another device: no remote copies, remote signals or barrier semaphores. Data moves between devices by JAX's collectives and lax.ppermute only.
A program may use at most 128 MiB of HBM per device.

v0:
```python
import jax
import jax.numpy as jnp
from jax import lax
from jax.sharding import PartitionSpec as P

EXPERTS = 32
CAP = 32


def running_rank(onehot):
    return jnp.sum((jnp.cumsum(onehot, axis=0) - onehot) * onehot, axis=1)


def local(
    attn_heads,
    w_out,
    residual,
    norm_gain,
    route_ids,
    route_weight,
    row_order,
    slot_expert,
    w_in,
    w_down,
):
    row_count = residual.shape[0]
    wide_count = lax.axis_size("wide")
    width_local = residual.shape[1]
    partial_terms = jnp.dot(attn_heads, w_out, preferred_element_type=jnp.float32)
    projected = lax.psum_scatter(
        partial_terms.astype(jnp.bfloat16), "narrow", scatter_dimension=1, tiled=True
    ).astype(jnp.float32)
    hidden = (residual.astype(jnp.float32) + projected).astype(jnp.bfloat16)
    whole_rows = lax.all_gather(hidden, "narrow", axis=1, tiled=True).astype(jnp.float32)
    mean_sq = jnp.mean(whole_rows * whole_rows, axis=1, keepdims=True)
    normed = (whole_rows * lax.rsqrt(mean_sq + 1e-06) * norm_gain).astype(jnp.bfloat16)
    slot_count = slot_expert.shape[0]
    slot_local = w_in.shape[0]
    top_count = route_ids.shape[1]
    model_width = normed.shape[1]
    held = (slot_expert[None, :] == jnp.arange(EXPERTS, dtype=jnp.int32)[:, None]).astype(jnp.int32)
    copies = jnp.sum(held, axis=1)
    replica_rank = jnp.cumsum(held, axis=1) - held
    flat_ids = route_ids.reshape(-1)
    choose_expert = (flat_ids[:, None] == jnp.arange(EXPERTS, dtype=jnp.int32)[None, :]).astype(
        jnp.int32
    )
    copy_count = jnp.sum(choose_expert * copies[None, :], axis=1)
    replica = jnp.repeat(row_order, top_count) % copy_count
    held_rows = jnp.sum(choose_expert[:, :, None] * held[None, :, :], axis=1)
    rank_rows = jnp.sum(choose_expert[:, :, None] * replica_rank[None, :, :], axis=1)
    slot_hit = held_rows * (rank_rows == replica[:, None]).astype(jnp.int32)
    slot_index = jnp.sum(slot_hit * jnp.arange(slot_count, dtype=jnp.int32)[None, :], axis=1)
    position = slot_index * CAP + running_rank(slot_hit)
    outgoing = (
        jnp.zeros((slot_count * CAP, model_width), jnp.bfloat16)
        .at[position]
        .set(jnp.repeat(normed, top_count, axis=0))
    )
    outgoing = outgoing.reshape(wide_count, slot_local, CAP, model_width)
    gate_up = jnp.einsum(
        "nscd,sghd->nscgh",
        lax.all_to_all(outgoing, "wide", split_axis=0, concat_axis=0, tiled=True),
        w_in,
        preferred_element_type=jnp.float32,
    )
    active = (jax.nn.relu(gate_up[:, :, :, 0, :]) * gate_up[:, :, :, 1, :]).astype(jnp.bfloat16)
    lowered = jnp.einsum("nsch,shd->nscd", active, w_down, preferred_element_type=jnp.float32)
    pieces = lowered.astype(jnp.bfloat16)
    summed = lax.psum_scatter(
        pieces.astype(jnp.float32).astype(jnp.bfloat16), "narrow", scatter_dimension=3, tiled=True
    )
    returned = lax.all_to_all(summed, "wide", split_axis=0, concat_axis=0, tiled=True)
    expert_out = returned.reshape(slot_count * CAP, width_local)[position]
    weighted = route_weight[:, :, None] * expert_out.reshape(
        row_count, top_count, width_local
    ).astype(jnp.float32)
    mixed = (hidden.astype(jnp.float32) + jnp.sum(weighted, axis=1)).astype(jnp.bfloat16)
    pair_rows = row_count // wide_count
    target_dev = row_order // row_count
    target_place = row_order % row_count
    choose_target = (
        target_dev[:, None] == jnp.arange(wide_count, dtype=jnp.int32)[None, :]
    ).astype(jnp.int32)
    packed_index = target_dev * pair_rows + running_rank(choose_target)
    packed = jnp.zeros((row_count, width_local), jnp.bfloat16).at[packed_index].set(mixed)
    places = jnp.zeros((row_count,), jnp.int32).at[packed_index].set(target_place)
    arrived_rows, arrived_places = (
        lax.all_to_all(
            packed.reshape(wide_count, pair_rows, width_local),
            "wide",
            split_axis=0,
            concat_axis=0,
            tiled=True,
        ),
        lax.all_to_all(
            places.reshape(wide_count, pair_rows), "wide", split_axis=0, concat_axis=0, tiled=True
        ),
    )
    return (
        jnp.zeros((row_count, width_local), jnp.bfloat16)
        .at[arrived_places.reshape(-1)]
        .set(arrived_rows.reshape(row_count, width_local))
    )


def solution(mesh):
    placed = (
        P("wide", "narrow"),
        P("narrow", None),
        P("wide", "narrow"),
        P(),
        P("wide", None),
        P("wide", None),
        P("wide"),
        P(),
        P("wide", None, "narrow", None),
        P("wide", "narrow", None),
    )
    return jax.shard_map(
        local, mesh=mesh, in_specs=placed, out_specs=P("wide", "narrow"), check_vma=False
    )
```

profile of v0, /device:TPU:1, one launch (start us, length us, event | category | flops | bytes accessed | tf_op | source)
XLA Modules:
  0.0 446.1 jit_solution(14987172049818661340)
XLA Ops:
  6.5 1.8 convolution_convert_fusion
  8.3 0.9 copy.29
  9.3 0.7 fusion.23
  10.0 0.2 reduce_window_sum.38
  10.2 0.8 fusion.24
  11.0 0.8 copy.24
  12.0 0.7 broadcast_in_dim.14
  12.7 0.1 reshape.232
  12.8 0.9 multiply_reduce_fusion.1
  13.8 0.1 add_select_fusion
  13.9 1.2 reduce-window.6
  15.2 0.2 slice_reduce_fusion
  15.4 0.1 multiply_reduce_fusion.3
  15.6 19.5 %reduce-scatter.7.cloned.1.call-done = bf16[384,128]{1,0:T(8,128)(2,1)} async-done(((bf16[1536,128]{1,0:T(8,128)(2,1)}), bf16[384,128]{1,0:T(8,128)(2,1)}) %reduce-scatter.7.cloned.1.call-update) | async-done | bytes 98320
  35.1 1.0 copy.30
  36.1 10.2 %all_gather.3 = bf16[128,1536]{1,0:T(8,128)(2,1)S(1)} all-gather(bf16[128,384]{1,0:T(8,128)(2,1)S(1)} %add_convert_fusion.1), channel_id=1, replica_groups=mesh['wide'=64,'narrow'=4] {'narrow'}, dimensions={1}, use_global_device_ids=true | all-gather | bytes 491520 | tf_op jit(solution)/shard_map/all_gather | solution.py:34
  46.3 0.2 fusion.12
  46.5 0.2 fusion.14
  46.7 0.4 broadcast_in_dim.16
  47.1 1.3 reshape.264
  48.4 7.7 %scatter_custom_fusion.1 = bf16[2048,1536]{1,0:T(8,128)(2,1)} fusion(s32[512]{0:T(512)S(1)} %bitcast.72, bf16[512,1536]{1,0:T(8,128)(2,1)} %reshape.264, bf16[]{:T(256)} %constant.53.clone.1), kind=kCustom, calls=%fused_computation.10 | custom fusion | bytes 6291968 | tf_op jit(solution)/shard_map/scatter | solution.py:58
  56.1 156.6 %all_to_all.24 = bf16[64,1,32,1536]{3,2,1,0:T(8,128)(2,1)S(1)} all-to-all(bf16[64,1,32,1536]{3,2,1,0:T(8,128)(2,1)} %bitcast.66), channel_id=1, replica_groups=mesh['wide'=64,'narrow'=4] {'wide'}, dimensions={0} | all-to-all | bytes 12582912 | tf_op jit(solution)/shard_map/all_to_all | solution.py:63
  212.7 3.7 fusion.4
  216.5 4.5 %convert_bitcast_fusion = bf16[64,1,32,1536]{3,2,0,1:T(8,128)(2,1)} fusion(f32[64,1,32,2,192]{4,2,3,0,1:T(8,128)S(1)} %fusion.4, bf16[1,192,1536]{2,1,0:T(8,128)(2,1)S(1)} %copy-done.2), kind=kOutput, calls=%fused_computation.7 | convolution fusion | flops 1212284928 | bytes 10027008 | tf_op jit(solution)/shard_map/nsch,shd->nscd/dot_general | solution.py:68
  221.0 33.7 %copy.31 = bf16[64,1,32,1536]{2,0,1,3:T(8,128)(2,1)} copy(bf16[64,1,32,1536]{3,2,0,1:T(8,128)(2,1)} %convert_bitcast_fusion) | data formatting | bytes 12582912
  254.7 33.1 %reshape.291 = bf16[1536,2048]{1,0:T(8,128)(2,1)} reshape(bf16[1536,1,64,32]{3,2,1,0:T(8,128)(2,1)} %bitcast.65) | data formatting | bytes 12582912
  287.8 0.6 copy-done.6
  288.5 0.2 reduce_window_sum.37
  288.7 0.2 select_reduce_fusion.1
  288.9 1.0 scatter_custom_fusion
  289.9 0.8 all_to_all.15
  290.6 5.8 %all-to-all-start = ((s32[64,1,2]{2,1,0:T(1,128)}), s32[64,1,2]{2,1,0:T(1,128)S(1)}, u32[]{:S(2)}, u32[]{:S(2)}) async-start(s32[64,1,2]{2,1,0:T(1,128)} %bitcast), calls=%async_computation | async-start | bytes 65536 | tf_op jit(solution)/shard_map/all_to_all | solution.py:96
  296.4 52.8 %reduce-scatter.9.cloned.1.call-done = bf16[384,2048]{1,0:T(8,128)(2,1)} async-done(((bf16[1536,2048]{1,0:T(8,128)(2,1)}), bf16[384,2048]{1,0:T(8,128)(2,1)}) %reduce-scatter.9.cloned.1.call-update) | async-done | bytes 1572880
  349.3 8.4 %reshape.292 = bf16[384,1,64,32]{3,2,1,0:T(8,128)(2,1)} reshape(bf16[384,2048]{1,0:T(8,128)(2,1)} %reduce-scatter.9.cloned.1.call-done) | data formatting | bytes 3145728
  357.6 8.7 %copy.32 = bf16[64,1,32,384]{3,2,0,1:T(8,128)(2,1)} copy(bf16[64,1,32,384]{2,0,1,3:T(8,128)(2,1)} %bitcast.67) | data formatting | bytes 3145728
  366.4 10.7 %all-to-all-start.2 = ((bf16[64,1,32,384]{3,2,1,0:T(8,128)(2,1)}), bf16[64,1,32,384]{3,2,1,0:T(8,128)(2,1)S(1)}, u32[]{:S(2)}, u32[]{:S(2)}) async-start(bf16[64,1,32,384]{3,2,1,0:T(8,128)(2,1)} %bitcast.69), calls=%async_computation.2 | async-start | bytes 3145728 | tf_op jit(solution)/shard_map/all_to_all | solution.py:73
  377.2 0.5 broadcast.212
  377.7 0.7 reduce.5
  378.5 0.1 reshape.231
  378.6 38.2 %all-to-all-done.2 = bf16[64,1,32,384]{3,2,1,0:T(8,128)(2,1)S(1)} async-done(((bf16[64,1,32,384]{3,2,1,0:T(8,128)(2,1)}), bf16[64,1,32,384]{3,2,1,0:T(8,128)(2,1)S(1)}, u32[]{:S(2)}, u32[]{:S(2)}) %all-to-all-start.2) | async-done | bytes 1572896 | tf_op jit(solution)/shard_map/all_to_all | solution.py:73
  416.8 1.9 gather_fusion
  418.8 0.2 reshape.243
  419.0 0.5 multiply_reduce_fusion.2
  419.5 1.1 scatter_custom_fusion.2
  420.6 0.7 reshape.241
  421.3 6.1 %all-to-all-start.3 = ((bf16[64,2,384]{2,1,0:T(2,128)(2,1)}), bf16[64,2,384]{2,1,0:T(2,128)(2,1)S(1)}, u32[]{:S(2)}, u32[]{:S(2)}) async-start(bf16[64,2,384]{2,1,0:T(2,128)(2,1)} %reshape.241), calls=%async_computation.3 | async-start | bytes 196608 | tf_op jit(solution)/shard_map/all_to_all | solution.py:89
  427.4 10.2 %all-to-all-done.3 = bf16[64,2,384]{2,1,0:T(2,128)(2,1)S(1)} async-done(((bf16[64,2,384]{2,1,0:T(2,128)(2,1)}), bf16[64,2,384]{2,1,0:T(2,128)(2,1)S(1)}, u32[]{:S(2)}, u32[]{:S(2)}) %all-to-all-start.3) | async-done | bytes 98336 | tf_op jit(solution)/shard_map/all_to_all | solution.py:89
  437.6 1.6 scatter_custom_fusion.3
  (36 shorter events, 0.7 us)
Async XLA Ops:
  6.5 206.2 %copy-start = (bf16[1,2,192,1536]{3,2,1,0:T(8,128)(2,1)S(1)}, bf16[1,2,192,1536]{3,2,1,0:T(8,128)(2,1)}, u32[]{:S(2)}) copy-start(bf16[1,2,192,1536]{3,2,1,0:T(8,128)(2,1)} %param.18) | copy-start | bytes 3538948
  6.5 29.5 %copy-start.3 = (bf16[128,384]{1,0:T(8,128)(2,1)S(1)}, bf16[128,384]{1,0:T(8,128)(2,1)}, u32[]{:S(2)}) copy-start(bf16[128,384]{1,0:T(8,128)(2,1)} %param.12) | copy-start | bytes 294916
  6.5 39.9 %copy-start.4 = (f32[1536]{0:T(1024)S(1)}, f32[1536]{0:T(1024)}, u32[]{:S(2)}) copy-start(f32[1536]{0:T(1024)} %param.13) | copy-start | bytes 18436
  6.5 28.5 %reduce-scatter.7.cloned.1.call-start = ((), (), s32[]{:S(2)}) async-start(), calls=%async_computation.6 | async-start | bytes 491520
  9.3 340.0 %reduce-scatter.9.cloned.1.call-start = ((), (), s32[]{:S(2)}) async-start(), calls=%async_computation.7 | async-start | bytes 7864320
  212.7 3.7 copy-start.2
  287.7 0.7 copy-start.6
  290.6 75.8 %all-to-all-start = ((s32[64,1,2]{2,1,0:T(1,128)}), s32[64,1,2]{2,1,0:T(1,128)S(1)}, u32[]{:S(2)}, u32[]{:S(2)}) async-start(s32[64,1,2]{2,1,0:T(1,128)} %bitcast), calls=%async_computation | async-start | bytes 65536 | tf_op jit(solution)/shard_map/all_to_all | solution.py:96
  357.6 19.4 %copy-start.5 = (f32[128,4]{0,1:T(4,128)S(1)}, f32[128,4]{0,1:T(4,128)}, u32[]{:S(2)}) copy-start(f32[128,4]{0,1:T(4,128)} %param.15) | copy-start | bytes 6148
  366.4 50.5 %all-to-all-start.2 = ((bf16[64,1,32,384]{3,2,1,0:T(8,128)(2,1)}), bf16[64,1,32,384]{3,2,1,0:T(8,128)(2,1)S(1)}, u32[]{:S(2)}, u32[]{:S(2)}) async-start(bf16[64,1,32,384]{3,2,1,0:T(8,128)(2,1)} %bitcast.69), calls=%async_computation.2 | async-start | bytes 3145728 | tf_op jit(solution)/shard_map/all_to_all | solution.py:73
  377.1 62.1 %copy-start.1 = (bf16[1,2,192,1536]{3,2,1,0:T(8,128)(2,1)S(1)}, bf16[1,2,192,1536]{3,2,1,0:T(8,128)(2,1)}, u32[]{:S(2)}) copy-start(bf16[1,2,192,1536]{3,2,1,0:T(8,128)(2,1)} %param.18) | copy-start | bytes 3538948
  421.3 16.3 %all-to-all-start.3 = ((bf16[64,2,384]{2,1,0:T(2,128)(2,1)}), bf16[64,2,384]{2,1,0:T(2,128)(2,1)S(1)}, u32[]{:S(2)}, u32[]{:S(2)}) async-start(bf16[64,2,384]{2,1,0:T(2,128)(2,1)} %reshape.241), calls=%async_computation.3 | async-start | bytes 196608 | tf_op jit(solution)/shard_map/all_to_all | solution.py:89
Sparse Core Ops, SparseCore 0:
  9.9 25.1 reduce-scatter.6
  287.9 61.3 reduce-scatter.8
where the time goes:
time: 448 us; the launch traced here: 446 us
  blocking collectives  167 us (37%)
  waiting for transfers between devices  121 us (27%)
  local copies, waits for them, and re-layouts  105 us (23%)
  starting transfers between devices  22.7 us (5%)
  between operations  13.7 us (3%)
  matrix products  10 us (2%)
  other arithmetic  7.34 us (2%)
    all_to_all x1, blocking collectives, local(): lax.all_to_all(outgoing, 'wide', split_axis=0, concat_axis=0, tiled=True)  157 us
    unnamed x22, local copies, waits for them, and re-layouts  87.3 us
    unnamed x4, waiting for transfers between devices  72.3 us
    all_to_all x1, waiting for transfers between devices, local(): lax.all_to_all(summed, 'wide', split_axis=0, concat_axis=0, tiled=True)  38.2 us
    all_to_all x1, starting transfers between devices, local(): lax.all_to_all(summed, 'wide', split_axis=0, concat_axis=0, tiled=True)  10.7 us
    all_gather x1, blocking collectives, local(): lax.all_gather(hidden, 'narrow', axis=1, tiled=True).astype(jnp.float32)  10.2 us
    all_to_all x1, waiting for transfers between devices, local(): lax.all_to_all(packed.reshape(wide_count, pair_rows, width_local), 'wide'...  10.2 us
  transfers between devices with their start and end apart: 5, of which 4 were waited for; matrix products, arithmetic and copies ran while one was open for 6% of the time, Pallas kernels for 0%

commit v1 on v0

--- a/solution.py
+++ b/solution.py
@@ -25,19 +25,30 @@
 ):
     row_count = residual.shape[0]
     wide_count = lax.axis_size("wide")
+    narrow_count = lax.axis_size("narrow")
     width_local = residual.shape[1]
+    model_width = width_local * narrow_count
+    me_narrow = lax.axis_index("narrow")
+
+    slot_local = w_in.shape[0]
+    hid_local = w_down.shape[1]
+    wd = w_down.reshape(slot_local, hid_local, narrow_count, width_local)
+    wd = jnp.moveaxis(wd, 2, 0)
+    wd_cols = lax.all_to_all(wd, "narrow", split_axis=0, concat_axis=0, tiled=True)
+
     partial_terms = jnp.dot(attn_heads, w_out, preferred_element_type=jnp.float32)
     projected = lax.psum_scatter(
         partial_terms.astype(jnp.bfloat16), "narrow", scatter_dimension=1, tiled=True
     ).astype(jnp.float32)
     hidden = (residual.astype(jnp.float32) + projected).astype(jnp.bfloat16)
-    whole_rows = lax.all_gather(hidden, "narrow", axis=1, tiled=True).astype(jnp.float32)
-    mean_sq = jnp.mean(whole_rows * whole_rows, axis=1, keepdims=True)
-    normed = (whole_rows * lax.rsqrt(mean_sq + 1e-06) * norm_gain).astype(jnp.bfloat16)
+    hidden_f = hidden.astype(jnp.float32)
+    sum_sq = lax.psum(jnp.sum(hidden_f * hidden_f, axis=1, keepdims=True), "narrow")
+    mean_sq = sum_sq / model_width
+    gain_local = lax.dynamic_slice_in_dim(norm_gain, me_narrow * width_local, width_local)
+    normed = (hidden_f * lax.rsqrt(mean_sq + 1e-06) * gain_local).astype(jnp.bfloat16)
+
     slot_count = slot_expert.shape[0]
-    slot_local = w_in.shape[0]
     top_count = route_ids.shape[1]
-    model_width = normed.shape[1]
     held = (slot_expert[None, :] == jnp.arange(EXPERTS, dtype=jnp.int32)[:, None]).astype(jnp.int32)
     copies = jnp.sum(held, axis=1)
     replica_rank = jnp.cumsum(held, axis=1) - held
@@ -53,29 +64,30 @@
     slot_index = jnp.sum(slot_hit * jnp.arange(slot_count, dtype=jnp.int32)[None, :], axis=1)
     position = slot_index * CAP + running_rank(slot_hit)
     outgoing = (
-        jnp.zeros((slot_count * CAP, model_width), jnp.bfloat16)
+        jnp.zeros((slot_count * CAP, width_local), jnp.bfloat16)
         .at[position]
         .set(jnp.repeat(normed, top_count, axis=0))
     )
-    outgoing = outgoing.reshape(wide_count, slot_local, CAP, model_width)
+    outgoing = outgoing.reshape(wide_count, slot_local, CAP, width_local)
+    arrived = lax.all_to_all(outgoing, "wide", split_axis=0, concat_axis=0, tiled=True)
+    whole = lax.all_gather(arrived, "narrow", axis=0, tiled=False)
+    w_in_q = w_in.reshape(slot_local, 2, hid_local, narrow_count, width_local)
     gate_up = jnp.einsum(
-        "nscd,sghd->nscgh",
-        lax.all_to_all(outgoing, "wide", split_axis=0, concat_axis=0, tiled=True),
-        w_in,
-        preferred_element_type=jnp.float32,
+        "pnscd,sghpd->nscgh", whole, w_in_q, preferred_element_type=jnp.float32
     )
     active = (jax.nn.relu(gate_up[:, :, :, 0, :]) * gate_up[:, :, :, 1, :]).astype(jnp.bfloat16)
-    lowered = jnp.einsum("nsch,shd->nscd", active, w_down, preferred_element_type=jnp.float32)
-    pieces = lowered.astype(jnp.bfloat16)
-    summed = lax.psum_scatter(
-        pieces.astype(jnp.float32).astype(jnp.bfloat16), "narrow", scatter_dimension=3, tiled=True
+    active_all = lax.all_gather(active, "narrow", axis=0, tiled=False)
+    lowered = jnp.einsum(
+        "qnsch,qshd->qnscd", active_all, wd_cols, preferred_element_type=jnp.float32
     )
+    pieces = lowered.astype(jnp.bfloat16).astype(jnp.float32)
+    summed = jnp.sum(pieces, axis=0).astype(jnp.bfloat16)
     returned = lax.all_to_all(summed, "wide", split_axis=0, concat_axis=0, tiled=True)
     expert_out = returned.reshape(slot_count * CAP, width_local)[position]
     weighted = route_weight[:, :, None] * expert_out.reshape(
         row_count, top_count, width_local
     ).astype(jnp.float32)
-    mixed = (hidden.astype(jnp.float32) + jnp.sum(weighted, axis=1)).astype(jnp.bfloat16)
+    mixed = (hidden_f + jnp.sum(weighted, axis=1)).astype(jnp.bfloat16)
     pair_rows = row_count // wide_count
     target_dev = row_order // row_count
     target_place = row_order % row_count

time: 448 us -> 309 us (0.69)
  blocking collectives: 167 us -> 61.2 us
  local copies, waits for them, and re-layouts: 105 us -> 18.2 us
  waiting for transfers between devices: 121 us -> 163 us
  starting transfers between devices: 22.7 us -> 32.5 us
    all_to_all x1, blocking collectives: 157 us -> 54.1 us  [local(): lax.all_to_all(outgoing, 'wide', split_axis=0, concat_axis=0, tiled=True)]
    all_gather x0 -> x2, waiting for transfers between devices: none -> 86.7 us  [the longest x1 60.7 us: local(): whole = lax.all_gather(arrived, 'narrow', axis=0, tiled=False)]
    unnamed x22 -> x20, local copies, waits for them, and re-layouts: 87.3 us -> 4.59 us
    unnamed x4, waiting for transfers between devices: 72.3 us -> 20.9 us
    all_gather x1 -> x0, blocking collectives: 10.2 us -> none  [local(): lax.all_gather(hidden, 'narrow', axis=1, tiled=True).astype(jnp.float32)]
    psum x0 -> x1, blocking collectives: none -> 7.1 us  [local(): lax.psum(jnp.sum(hidden_f * hidden_f, axis=1, keepdims=True), 'narrow')]
    all_to_all x0 -> x1, waiting for transfers between devices: none -> 6.99 us  [local(): lax.all_to_all(wd, 'narrow', split_axis=0, concat_axis=0, tiled=True)]
    all_to_all x1, starting transfers between devices: 5.83 us -> 11.9 us  [local(): lax.all_to_all(places.reshape(wide_count, pair_rows), 'wide', split_axis=...]
  transfers between devices with their start and end apart: 5 -> 7, of which waited for: 4 -> 6; matrix products, arithmetic and copies ran while one was open for 6% -> 5% of each run, Pallas kernels for 0% -> 0%
where the time goes in v1:
time: 309 us
  waiting for transfers between devices  163 us (53%)
  blocking collectives  61.2 us (20%)
  starting transfers between devices  32.5 us (11%)
  local copies, waits for them, and re-layouts  18.2 us (6%)
  between operations  13.4 us (4%)
  matrix products  13.2 us (4%)
  other arithmetic  7.4 us (2%)
    all_gather x1, waiting for transfers between devices, local(): whole = lax.all_gather(arrived, 'narrow', axis=0, tiled=False)  60.7 us
    all_to_all x1, blocking collectives, local(): lax.all_to_all(outgoing, 'wide', split_axis=0, concat_axis=0, tiled=True)  54.1 us
    all_to_all x1, waiting for transfers between devices, local(): lax.all_to_all(summed, 'wide', split_axis=0, concat_axis=0, tiled=True)  38.2 us
    all_gather x1, waiting for transfers between devices, local(): active_all = lax.all_gather(active, 'narrow', axis=0, tiled=False)  25.9 us
    unnamed x4, waiting for transfers between devices  20.9 us
    all_to_all x1, starting transfers between devices, local(): lax.all_to_all(places.reshape(wide_count, pair_rows), 'wide', split_axis=...  11.9 us
    all_to_all x1, starting transfers between devices, local(): lax.all_to_all(summed, 'wide', split_axis=0, concat_axis=0, tiled=True)  10.9 us
    all_to_all x1, waiting for transfers between devices, local(): lax.all_to_all(packed.reshape(wide_count, pair_rows, width_local), 'wide'...  10.2 us
  transfers between devices with their start and end apart: 7, of which 6 were waited for; matrix products, arithmetic and copies ran while one was open for 5% of the time, Pallas kernels for 0%

profile of v1, /device:TPU:1, one launch (start us, length us, event | category | flops | bytes accessed | tf_op | source)
XLA Modules:
  0.0 308.9 jit_solution(12603089173667754185)
XLA Ops:
  6.6 1.2 copy-done
  7.8 1.3 convolution_convert_fusion
  9.1 0.9 copy.43
  10.1 0.2 reduce_window_sum.38
  10.3 0.1 fusion.25
  10.4 0.1 copy.31
  10.8 0.1 reshape.256
  11.0 0.9 multiply_reduce_fusion.1
  11.9 0.1 add_select_fusion
  12.1 1.2 reduce-window.6
  13.3 0.2 slice_reduce_fusion
  13.6 0.8 dynamic_slice.3
  14.5 20.9 %reduce-scatter.4.cloned.1.call-done = bf16[384,128]{1,0:T(8,128)(2,1)} async-done(((bf16[1536,128]{1,0:T(8,128)(2,1)}), bf16[384,128]{1,0:T(8,128)(2,1)}) %reduce-scatter.4.cloned.1.call-update) | async-done | bytes 98320
  35.3 1.0 copy.44
  36.4 0.1 fusion.12
  36.5 7.1 %psum.7 = f32[128,1]{0,1:T(1,128)S(1)} all-reduce(f32[128,1]{0,1:T(1,128)S(1)} %bitcast.69), channel_id=1, replica_groups=mesh['wide'=64,'narrow'=4] {'narrow'}, use_global_device_ids=true, to_apply=%region_14.15 | all-reduce | flops 128 | bytes 1024 | tf_op jit(solution)/shard_map/psum | solution.py:45
  43.9 2.9 scatter_custom_fusion.1
  46.8 54.1 %all_to_all.29 = bf16[64,1,32,384]{3,2,1,0:T(8,128)(2,1)} all-to-all(bf16[64,1,32,384]{3,2,1,0:T(8,128)(2,1)S(1)} %bitcast.61), channel_id=1, replica_groups=mesh['wide'=64,'narrow'=4] {'wide'}, dimensions={0} | all-to-all | bytes 3145728 | tf_op jit(solution)/shard_map/all_to_all | solution.py:72
  101.0 1.2 copy-done.1
  102.2 1.3 reshape.262
  103.4 60.7 %all-gather.5.cloned.1.call-done = bf16[256,1,32,384]{3,2,1,0:T(8,128)(2,1)} async-done(((bf16[64,1,32,384]{3,2,1,0:T(8,128)(2,1)}), bf16[256,1,32,384]{3,2,1,0:T(8,128)(2,1)}) %all-gather.5.cloned.1.call-update) | async-done | bytes 6291472 | tf_op jit(solution)/shard_map/all_gather | solution.py:73
  164.2 5.9 %fusion.2 = f32[64,1,32,2,192]{4,2,3,0,1:T(8,128)S(1)} fusion(bf16[4,64,32,384,1]{3,2,1,0,4:T(8,128)(2,1)} %bitcast.70, bf16[2,192,4,384]{3,2,1,0:T(4,128)(2,1)} %reshape.262), kind=kOutput, calls=%fused_computation.11 | convolution fusion | flops 2415919104 | bytes 10616832 | tf_op jit(solution)/shard_map/pnscd,sghpd->nscgh/dot_general | solution.py:75
  170.0 1.5 fusion.8
  171.6 0.1 reshape.264
  171.8 0.9 copy.37
  172.7 3.5 %all-to-all-start.2 = ((bf16[4,1,192,384]{3,2,1,0:T(8,128)(2,1)}), bf16[4,1,192,384]{3,2,1,0:T(8,128)(2,1)S(1)}, u32[]{:S(2)}, u32[]{:S(2)}) async-start(bf16[4,1,192,384]{3,2,1,0:T(8,128)(2,1)} %copy.37), calls=%async_computation.2 | async-start | bytes 1179648 | tf_op jit(solution)/shard_map/all_to_all | solution.py:37
  176.3 0.2 reduce_window_sum.37
  176.4 0.2 select_reduce_fusion.1
  176.6 1.0 scatter_custom_fusion
  177.6 0.8 all_to_all.18
  178.4 7.0 %all-to-all-done.2 = bf16[4,1,192,384]{3,2,1,0:T(8,128)(2,1)S(1)} async-done(((bf16[4,1,192,384]{3,2,1,0:T(8,128)(2,1)}), bf16[4,1,192,384]{3,2,1,0:T(8,128)(2,1)S(1)}, u32[]{:S(2)}, u32[]{:S(2)}) %all-to-all-start.2) | async-done | bytes 589856 | tf_op jit(solution)/shard_map/all_to_all | solution.py:37
  185.4 11.9 %all-to-all-start = ((s32[64,1,2]{2,1,0:T(1,128)}), s32[64,1,2]{2,1,0:T(1,128)S(1)}, u32[]{:S(2)}, u32[]{:S(2)}) async-start(s32[64,1,2]{2,1,0:T(1,128)} %bitcast), calls=%async_computation | async-start | bytes 65536 | tf_op jit(solution)/shard_map/all_to_all | solution.py:108
  197.2 25.9 %all-gather.7.cloned.1.call-done = bf16[256,1,32,1,192]{4,2,3,1,0:T(8,128)(2,1)} async-done(((bf16[64,1,32,1,192]{4,2,3,1,0:T(8,128)(2,1)}), bf16[256,1,32,1,192]{4,2,3,1,0:T(8,128)(2,1)}) %all-gather.7.cloned.1.call-update) | async-done | bytes 3145744 | tf_op jit(solution)/shard_map/all_gather | solution.py:79
  223.2 6.1 %convert_reduce_fusion = bf16[64,32,384]{2,1,0:T(8,128)(2,1)} fusion(bf16[4,64,32,192]{3,2,1,0:T(8,128)(2,1)} %bitcast.71, bf16[4,1,192,384]{3,2,1,0:T(8,128)(2,1)S(1)} %all-to-all-done.2), kind=kOutput, calls=%fused_computation.7 | convolution fusion | flops 1213464576 | bytes 5308416 | tf_op jit(solution)/shard_map/qnsch,qshd->qnscd/dot_general | solution.py:80
  229.3 10.9 %all-to-all-start.3 = ((bf16[64,1,32,384]{3,2,1,0:T(8,128)(2,1)}), bf16[64,1,32,384]{3,2,1,0:T(8,128)(2,1)S(1)}, u32[]{:S(2)}, u32[]{:S(2)}) async-start(bf16[64,1,32,384]{3,2,1,0:T(8,128)(2,1)} %bitcast.63), calls=%async_computation.3 | async-start | bytes 3145728 | tf_op jit(solution)/shard_map/all_to_all | solution.py:85
  240.2 0.1 copy.30
  240.3 0.5 broadcast.209
  240.9 0.7 reduce.10
  241.6 0.1 reshape.255
  241.7 38.2 %all-to-all-done.3 = bf16[64,1,32,384]{3,2,1,0:T(8,128)(2,1)S(1)} async-done(((bf16[64,1,32,384]{3,2,1,0:T(8,128)(2,1)}), bf16[64,1,32,384]{3,2,1,0:T(8,128)(2,1)S(1)}, u32[]{:S(2)}, u32[]{:S(2)}) %all-to-all-start.3) | async-done | bytes 1572896 | tf_op jit(solution)/shard_map/all_to_all | solution.py:85
  280.0 1.9 gather_fusion
  281.9 0.2 reshape.269
  282.1 0.5 multiply_reduce_fusion.2
  282.6 1.1 scatter_custom_fusion.2
  283.7 0.7 reshape.267
  284.4 6.1 %all-to-all-start.4 = ((bf16[64,2,384]{2,1,0:T(2,128)(2,1)}), bf16[64,2,384]{2,1,0:T(2,128)(2,1)S(1)}, u32[]{:S(2)}, u32[]{:S(2)}) async-start(bf16[64,2,384]{2,1,0:T(2,128)(2,1)} %reshape.267), calls=%async_computation.4 | async-start | bytes 196608 | tf_op jit(solution)/shard_map/all_to_all | solution.py:101
  290.5 10.2 %all-to-all-done.4 = bf16[64,2,384]{2,1,0:T(2,128)(2,1)S(1)} async-done(((bf16[64,2,384]{2,1,0:T(2,128)(2,1)}), bf16[64,2,384]{2,1,0:T(2,128)(2,1)S(1)}, u32[]{:S(2)}, u32[]{:S(2)}) %all-to-all-start.4) | async-done | bytes 98336 | tf_op jit(solution)/shard_map/all_to_all | solution.py:101
  300.7 1.6 scatter_custom_fusion.3
  (43 shorter events, 1.1 us)
Async XLA Ops:
  6.5 1.3 copy-start
  6.5 3.5 %copy-start.4 = (s32[64]{0:T(128)S(1)}, s32[64]{0:T(128)}, u32[]{:S(2)}) copy-start(s32[64]{0:T(128)} %param.17) | copy-start | bytes 772
  6.5 3.9 %copy-start.5 = (s32[128,4]{0,1:T(4,128)S(1)}, s32[128,4]{0,1:T(4,128)}, u32[]{:S(2)}) copy-start(s32[128,4]{0,1:T(4,128)} %param.14) | copy-start | bytes 6148
  6.5 4.2 %copy-start.7 = (s32[128]{0:T(128)S(1)}, s32[128]{0:T(128)}, u32[]{:S(2)}) copy-start(s32[128]{0:T(128)} %param.16) | copy-start | bytes 1540
  6.5 28.8 %reduce-scatter.4.cloned.1.call-start = ((), (), s32[]{:S(2)}) async-start(), calls=%async_computation.8 | async-start | bytes 491520
  9.1 27.3 %copy-start.2 = (bf16[128,384]{1,0:T(8,128)(2,1)S(1)}, bf16[128,384]{1,0:T(8,128)(2,1)}, u32[]{:S(2)}) copy-start(bf16[128,384]{1,0:T(8,128)(2,1)} %param.12) | copy-start | bytes 294916
  10.0 154.1 %all-gather.5.cloned.1.call-start = ((), (), s32[]{:S(2)}) async-start(), calls=%async_computation.6 | async-start | bytes 7864320 | tf_op jit(solution)/shard_map/all_gather | solution.py:73
  100.9 1.3 copy-start.1
  100.9 122.3 %all-gather.7.cloned.1.call-start = ((), (), s32[]{:S(2)}) async-start(), calls=%async_computation.7 | async-start | bytes 5242880 | tf_op jit(solution)/shard_map/all_gather | solution.py:79
  170.0 1.6 copy-start.3
  172.7 12.7 %all-to-all-start.2 = ((bf16[4,1,192,384]{3,2,1,0:T(8,128)(2,1)}), bf16[4,1,192,384]{3,2,1,0:T(8,128)(2,1)S(1)}, u32[]{:S(2)}, u32[]{:S(2)}) async-start(bf16[4,1,192,384]{3,2,1,0:T(8,128)(2,1)} %copy.37), calls=%async_computation.2 | async-start | bytes 1179648 | tf_op jit(solution)/shard_map/all_to_all | solution.py:37
  185.4 43.9 %all-to-all-start = ((s32[64,1,2]{2,1,0:T(1,128)}), s32[64,1,2]{2,1,0:T(1,128)S(1)}, u32[]{:S(2)}, u32[]{:S(2)}) async-start(s32[64,1,2]{2,1,0:T(1,128)} %bitcast), calls=%async_computation | async-start | bytes 65536 | tf_op jit(solution)/shard_map/all_to_all | solution.py:108
  229.3 11.0 %copy-start.6 = (f32[128,4]{0,1:T(4,128)S(1)}, f32[128,4]{0,1:T(4,128)}, u32[]{:S(2)}) copy-start(f32[128,4]{0,1:T(4,128)} %param.15) | copy-start | bytes 6148
  229.3 50.7 %all-to-all-start.3 = ((bf16[64,1,32,384]{3,2,1,0:T(8,128)(2,1)}), bf16[64,1,32,384]{3,2,1,0:T(8,128)(2,1)S(1)}, u32[]{:S(2)}, u32[]{:S(2)}) async-start(bf16[64,1,32,384]{3,2,1,0:T(8,128)(2,1)} %bitcast.63), calls=%async_computation.3 | async-start | bytes 3145728 | tf_op jit(solution)/shard_map/all_to_all | solution.py:85
  284.4 16.3 %all-to-all-start.4 = ((bf16[64,2,384]{2,1,0:T(2,128)(2,1)}), bf16[64,2,384]{2,1,0:T(2,128)(2,1)S(1)}, u32[]{:S(2)}, u32[]{:S(2)}) async-start(bf16[64,2,384]{2,1,0:T(2,128)(2,1)} %reshape.267), calls=%async_computation.4 | async-start | bytes 196608 | tf_op jit(solution)/shard_map/all_to_all | solution.py:101
Sparse Core Ops, SparseCore 0:
  10.1 25.1 reduce-scatter.3
  101.0 63.0 all-gather.4
  171.7 51.4 all-gather.6

commit v2 on v1

--- a/solution.py
+++ b/solution.py
@@ -31,10 +31,8 @@
     me_narrow = lax.axis_index("narrow")
 
     slot_local = w_in.shape[0]
-    hid_local = w_down.shape[1]
-    wd = w_down.reshape(slot_local, hid_local, narrow_count, width_local)
-    wd = jnp.moveaxis(wd, 2, 0)
-    wd_cols = lax.all_to_all(wd, "narrow", split_axis=0, concat_axis=0, tiled=True)
+    w_in_all = lax.all_gather(w_in, "narrow", axis=0, tiled=False)
+    w_down_all = lax.all_gather(w_down, "narrow", axis=0, tiled=False)
 
     partial_terms = jnp.dot(attn_heads, w_out, preferred_element_type=jnp.float32)
     projected = lax.psum_scatter(
@@ -42,13 +40,13 @@
     ).astype(jnp.float32)
     hidden = (residual.astype(jnp.float32) + projected).astype(jnp.bfloat16)
     hidden_f = hidden.astype(jnp.float32)
-    sum_sq = lax.psum(jnp.sum(hidden_f * hidden_f, axis=1, keepdims=True), "narrow")
-    mean_sq = sum_sq / model_width
-    gain_local = lax.dynamic_slice_in_dim(norm_gain, me_narrow * width_local, width_local)
-    normed = (hidden_f * lax.rsqrt(mean_sq + 1e-06) * gain_local).astype(jnp.bfloat16)
+    whole_rows = lax.all_gather(hidden, "narrow", axis=1, tiled=True).astype(jnp.float32)
+    mean_sq = jnp.mean(whole_rows * whole_rows, axis=1, keepdims=True)
+    normed = (whole_rows * lax.rsqrt(mean_sq + 1e-06) * norm_gain).astype(jnp.bfloat16)
 
     slot_count = slot_expert.shape[0]
     top_count = route_ids.shape[1]
+    band = CAP // narrow_count
     held = (slot_expert[None, :] == jnp.arange(EXPERTS, dtype=jnp.int32)[:, None]).astype(jnp.int32)
     copies = jnp.sum(held, axis=1)
     replica_rank = jnp.cumsum(held, axis=1) - held
@@ -62,26 +60,30 @@
     rank_rows = jnp.sum(choose_expert[:, :, None] * replica_rank[None, :, :], axis=1)
     slot_hit = held_rows * (rank_rows == replica[:, None]).astype(jnp.int32)
     slot_index = jnp.sum(slot_hit * jnp.arange(slot_count, dtype=jnp.int32)[None, :], axis=1)
-    position = slot_index * CAP + running_rank(slot_hit)
+    rank = running_rank(slot_hit)
+    position = slot_index * CAP + rank
+    send_at = jnp.where(
+        rank // band == me_narrow, slot_index * band + rank % band, slot_count * band
+    )
     outgoing = (
-        jnp.zeros((slot_count * CAP, width_local), jnp.bfloat16)
-        .at[position]
-        .set(jnp.repeat(normed, top_count, axis=0))
+        jnp.zeros((slot_count * band, model_width), jnp.bfloat16)
+        .at[send_at]
+        .set(jnp.repeat(normed, top_count, axis=0), mode="drop")
     )
-    outgoing = outgoing.reshape(wide_count, slot_local, CAP, width_local)
+    outgoing = outgoing.reshape(wide_count, slot_local, band, model_width)
     arrived = lax.all_to_all(outgoing, "wide", split_axis=0, concat_axis=0, tiled=True)
-    whole = lax.all_gather(arrived, "narrow", axis=0, tiled=False)
-    w_in_q = w_in.reshape(slot_local, 2, hid_local, narrow_count, width_local)
     gate_up = jnp.einsum(
-        "pnscd,sghpd->nscgh", whole, w_in_q, preferred_element_type=jnp.float32
+        "nscd,qsghd->nscgqh", arrived, w_in_all, preferred_element_type=jnp.float32
     )
-    active = (jax.nn.relu(gate_up[:, :, :, 0, :]) * gate_up[:, :, :, 1, :]).astype(jnp.bfloat16)
-    active_all = lax.all_gather(active, "narrow", axis=0, tiled=False)
+    active = (jax.nn.relu(gate_up[:, :, :, 0]) * gate_up[:, :, :, 1]).astype(jnp.bfloat16)
     lowered = jnp.einsum(
-        "qnsch,qshd->qnscd", active_all, wd_cols, preferred_element_type=jnp.float32
+        "nscqh,qshd->qnscd", active, w_down_all, preferred_element_type=jnp.float32
     )
     pieces = lowered.astype(jnp.bfloat16).astype(jnp.float32)
     summed = jnp.sum(pieces, axis=0).astype(jnp.bfloat16)
+    summed = summed.reshape(wide_count, slot_local, band, narrow_count, width_local)
+    summed = lax.all_to_all(summed, "narrow", split_axis=3, concat_axis=2, tiled=True)
+    summed = summed.reshape(wide_count, slot_local, CAP, width_local)
     returned = lax.all_to_all(summed, "wide", split_axis=0, concat_axis=0, tiled=True)
     expert_out = returned.reshape(slot_count * CAP, width_local)[position]
     weighted = route_weight[:, :, None] * expert_out.reshape(

time: 309 us -> 262 us (0.85)
  blocking collectives: 61.2 us -> 10.2 us
  waiting for transfers between devices: 163 us -> 151 us
  starting transfers between devices: 32.5 us -> 42.3 us
  local copies, waits for them, and re-layouts: 18.2 us -> 23.4 us
    all_gather x2, waiting for transfers between devices: 86.7 us -> 15.3 us  [the longest x1 15.3 us: local(): w_down_all = lax.all_gather(w_down, 'narrow', axis=0, tiled=False)]
    all_to_all x1 -> x0, blocking collectives: 54.1 us -> none  [local(): lax.all_to_all(outgoing, 'wide', split_axis=0, concat_axis=0, tiled=True)]
    all_to_all x1 -> x2, waiting for transfers between devices: 6.99 us -> 56.7 us  [the longest x1 39 us: local(): lax.all_to_all(outgoing, 'wide', split_axis=0, concat_axis=0, tiled=True)]
    all_to_all x1 -> x2, starting transfers between devices: 3.48 us -> 19.5 us  [the longest x1 15.7 us: local(): lax.all_to_all(outgoing, 'wide', split_axis=0, concat_axis=0, tiled=True)]
    all_gather x0 -> x1, blocking collectives: none -> 10.2 us  [local(): lax.all_gather(hidden, 'narrow', axis=1, tiled=True).astype(jnp.float32)]
    all_to_all x1, waiting for transfers between devices: 0.01 us -> 7.92 us  [local(): lax.all_to_all(places.reshape(wide_count, pair_rows), 'wide', split_axis=...]
    psum x1 -> x0, blocking collectives: 7.1 us -> none  [local(): lax.psum(jnp.sum(hidden_f * hidden_f, axis=1, keepdims=True), 'narrow')]
    all_to_all x1, starting transfers between devices: 10.9 us -> 4.91 us  [local(): lax.all_to_all(summed, 'wide', split_axis=0, concat_axis=0, tiled=True)]
  transfers between devices with their start and end apart: 7 -> 8, of which waited for: 6 -> 7; matrix products, arithmetic and copies ran while one was open for 5% -> 9% of each run, Pallas kernels for 0% -> 0%
where the time goes in v2:
time: 262 us; the launch traced here: 261 us
  waiting for transfers between devices  151 us (58%)
  starting transfers between devices  42.3 us (16%)
  local copies, waits for them, and re-layouts  23.4 us (9%)
  matrix products  15.1 us (6%)
  between operations  13.4 us (5%)
  blocking collectives  10.2 us (4%)
  other arithmetic  6.04 us (2%)
    all_to_all x1, waiting for transfers between devices, local(): lax.all_to_all(outgoing, 'wide', split_axis=0, concat_axis=0, tiled=True)  39 us
    all_to_all x1, waiting for transfers between devices, local(): lax.all_to_all(summed, 'wide', split_axis=0, concat_axis=0, tiled=True)  38.3 us
    unnamed x4, waiting for transfers between devices  22.3 us
    all_to_all x1, waiting for transfers between devices, local(): lax.all_to_all(summed, 'narrow', split_axis=3, concat_axis=2, tiled=True)  17.7 us
    all_to_all x1, starting transfers between devices, local(): lax.all_to_all(outgoing, 'wide', split_axis=0, concat_axis=0, tiled=True)  15.7 us
    all_gather x1, waiting for transfers between devices, local(): w_down_all = lax.all_gather(w_down, 'narrow', axis=0, tiled=False)  15.3 us
    all_to_all x1, starting transfers between devices, local(): lax.all_to_all(places.reshape(wide_count, pair_rows), 'wide', split_axis=...  11.7 us
    all_gather x1, blocking collectives, local(): lax.all_gather(hidden, 'narrow', axis=1, tiled=True).astype(jnp.float32)  10.2 us
  transfers between devices with their start and end apart: 8, of which 7 were waited for; matrix products, arithmetic and copies ran while one was open for 9% of the time, Pallas kernels for 0%

profile of v2, /device:TPU:1, one launch (start us, length us, event | category | flops | bytes accessed | tf_op | source)
XLA Modules:
  0.0 261.0 jit_solution(4068019235683162514)
XLA Ops:
  6.5 1.3 copy-done
  7.8 1.3 convolution_convert_fusion
  9.1 0.9 copy.44
  10.1 0.7 all-gather.5.cloned.1.call-update
  11.3 0.2 reduce_window_sum.38
  11.8 0.9 multiply_reduce_fusion.1
  12.7 0.1 add_select_fusion
  12.9 1.2 reduce-window.6
  14.1 0.2 slice_reduce_fusion
  14.3 0.1 fusion.15
  14.5 20.9 %reduce-scatter.4.cloned.1.call-done = bf16[384,128]{1,0:T(8,128)(2,1)} async-done(((bf16[1536,128]{1,0:T(8,128)(2,1)}), bf16[384,128]{1,0:T(8,128)(2,1)}) %reduce-scatter.4.cloned.1.call-update) | async-done | bytes 98320
  35.4 1.0 copy.45
  36.4 10.2 %all_gather.15 = bf16[128,1536]{1,0:T(8,128)(2,1)S(1)} all-gather(bf16[128,384]{1,0:T(8,128)(2,1)S(1)} %add_convert_fusion.1), channel_id=1, replica_groups=mesh['wide'=64,'narrow'=4] {'narrow'}, dimensions={1}, use_global_device_ids=true | all-gather | bytes 491520 | tf_op jit(solution)/shard_map/all_gather | solution.py:43
  46.6 0.2 fusion.10
  46.8 0.2 fusion.12
  47.0 0.4 broadcast_in_dim.24
  47.4 1.3 reshape.372
  48.7 5.1 %scatter_custom_fusion.1 = bf16[512,1536]{1,0:T(8,128)(2,1)} fusion(s32[512]{0:T(512)S(1)} %bitcast.75, bf16[512,1536]{1,0:T(8,128)(2,1)} %reshape.372, bf16[]{:T(256)} %constant.82.clone.1), kind=kCustom, calls=%fused_computation.26 | custom fusion | bytes 1573376 | tf_op jit(solution)/shard_map/scatter | solution.py:71
  53.8 15.7 %all-to-all-start.1 = ((bf16[64,1,8,1536]{3,2,1,0:T(8,128)(2,1)}), bf16[64,1,8,1536]{3,2,1,0:T(8,128)(2,1)S(1)}, u32[]{:S(2)}, u32[]{:S(2)}) async-start(bf16[64,1,8,1536]{3,2,1,0:T(8,128)(2,1)} %bitcast.7), calls=%async_computation.1 | async-start | bytes 3145728 | tf_op jit(solution)/shard_map/all_to_all | solution.py:74
  69.6 0.7 all-gather.7.cloned.1.call-update
  70.3 39.0 %all-to-all-done.1 = bf16[64,1,8,1536]{3,2,1,0:T(8,128)(2,1)S(1)} async-done(((bf16[64,1,8,1536]{3,2,1,0:T(8,128)(2,1)}), bf16[64,1,8,1536]{3,2,1,0:T(8,128)(2,1)S(1)}, u32[]{:S(2)}, u32[]{:S(2)}) %all-to-all-start.1) | async-done | bytes 1572896 | tf_op jit(solution)/shard_map/all_to_all | solution.py:74
  109.3 7.6 %fusion.3 = f32[64,1,8,2,4,192]{5,2,3,4,0,1:T(8,128)} fusion(bf16[4,2,192,1536]{3,2,1,0:T(8,128)(2,1)} %all-gather.5.cloned.1.call-done, bf16[64,1,8,1536]{3,2,1,0:T(8,128)(2,1)S(1)} %all-to-all-done.1), kind=kOutput, calls=%fused_computation.12 | convolution fusion | flops 2415919104 | bytes 9437184 | tf_op jit(solution)/shard_map/nscd,qsghd->nscgqh/dot_general | solution.py:75
  116.9 15.3 %all-gather.7.cloned.1.call-done = bf16[4,192,1536]{2,1,0:T(8,128)(2,1)} async-done(((bf16[1,192,1536]{2,1,0:T(8,128)(2,1)}), bf16[4,192,1536]{2,1,0:T(8,128)(2,1)}) %all-gather.7.cloned.1.call-update) | async-done | bytes 2359312 | tf_op jit(solution)/shard_map/all_gather | solution.py:35
  132.2 6.2 %convert_reduce_fusion = bf16[64,8,1536]{2,1,0:T(8,128)(2,1)} fusion(bf16[4,192,1536]{2,1,0:T(8,128)(2,1)} %all-gather.7.cloned.1.call-done, f32[64,1,8,2,4,192]{5,2,3,4,0,1:T(8,128)} %fusion.3), kind=kOutput, calls=%fused_computation.5 | convolution fusion | flops 1214644224 | bytes 7077888 | tf_op jit(solution)/shard_map/nscqh,qshd->qnscd/dot_general | solution.py:79
  138.4 3.0 %reshape.346 = bf16[64,1,8,4,384]{4,3,2,0,1:T(4,128)(2,1)S(1)} reshape(bf16[64,8,1536]{2,1,0:T(8,128)(2,1)} %convert_reduce_fusion) | data formatting | bytes 3145728 | tf_op jit(solution)/shard_map/reshape | solution.py:84
  141.4 1.4 copy.39
  142.7 3.7 %all-to-all-start.2 = ((bf16[64,1,8,4,384]{4,2,0,1,3:T(8,128)(2,1)}), bf16[64,1,8,4,384]{4,2,0,1,3:T(8,128)(2,1)S(1)}, u32[]{:S(2)}, u32[]{:S(2)}) async-start(bf16[64,1,8,4,384]{4,2,0,1,3:T(8,128)(2,1)} %copy.39), calls=%async_computation.2 | async-start | bytes 3145728 | tf_op jit(solution)/shard_map/all_to_all | solution.py:85
  146.6 0.2 reduce_window_sum.37
  146.7 0.2 select_reduce_fusion.1
  146.9 1.0 scatter_custom_fusion
  147.9 0.8 all_to_all.26
  148.7 17.7 %all-to-all-done.2 = bf16[64,1,8,4,384]{4,2,0,1,3:T(8,128)(2,1)S(1)} async-done(((bf16[64,1,8,4,384]{4,2,0,1,3:T(8,128)(2,1)}), bf16[64,1,8,4,384]{4,2,0,1,3:T(8,128)(2,1)S(1)}, u32[]{:S(2)}, u32[]{:S(2)}) %all-to-all-start.2) | async-done | bytes 1572896 | tf_op jit(solution)/shard_map/all_to_all | solution.py:85
  166.4 11.7 %all-to-all-start = ((s32[64,1,2]{2,1,0:T(1,128)}), s32[64,1,2]{2,1,0:T(1,128)S(1)}, u32[]{:S(2)}, u32[]{:S(2)}) async-start(s32[64,1,2]{2,1,0:T(1,128)} %bitcast), calls=%async_computation | async-start | bytes 65536 | tf_op jit(solution)/shard_map/all_to_all | solution.py:110
  178.1 1.3 copy.53
  179.4 7.9 %all-to-all-done = s32[64,1,2]{2,1,0:T(1,128)S(1)} async-done(((s32[64,1,2]{2,1,0:T(1,128)}), s32[64,1,2]{2,1,0:T(1,128)S(1)}, u32[]{:S(2)}, u32[]{:S(2)}) %all-to-all-start) | async-done | bytes 544 | tf_op jit(solution)/shard_map/all_to_all | solution.py:110
  187.3 4.9 %all-to-all-start.3 = ((bf16[64,1,32,384]{3,2,1,0:T(8,128)(2,1)}), bf16[64,1,32,384]{3,2,1,0:T(8,128)(2,1)S(1)}, u32[]{:S(2)}, u32[]{:S(2)}) async-start(bf16[64,1,32,384]{3,2,1,0:T(8,128)(2,1)} %bitcast.68), calls=%async_computation.3 | async-start | bytes 3145728 | tf_op jit(solution)/shard_map/all_to_all | solution.py:87
  192.4 0.5 broadcast.319
  192.9 0.7 reduce.10
  193.6 0.1 reshape.337
  193.8 38.3 %all-to-all-done.3 = bf16[64,1,32,384]{3,2,1,0:T(8,128)(2,1)S(1)} async-done(((bf16[64,1,32,384]{3,2,1,0:T(8,128)(2,1)}), bf16[64,1,32,384]{3,2,1,0:T(8,128)(2,1)S(1)}, u32[]{:S(2)}, u32[]{:S(2)}) %all-to-all-start.3) | async-done | bytes 1572896 | tf_op jit(solution)/shard_map/all_to_all | solution.py:87
  232.1 1.9 gather_fusion
  234.0 0.2 reshape.351
  234.2 0.5 multiply_reduce_fusion.2
  234.7 1.1 scatter_custom_fusion.2
  235.8 0.7 reshape.349
  236.5 6.2 %all-to-all-start.4 = ((bf16[64,2,384]{2,1,0:T(2,128)(2,1)}), bf16[64,2,384]{2,1,0:T(2,128)(2,1)S(1)}, u32[]{:S(2)}, u32[]{:S(2)}) async-start(bf16[64,2,384]{2,1,0:T(2,128)(2,1)} %reshape.349), calls=%async_computation.4 | async-start | bytes 196608 | tf_op jit(solution)/shard_map/all_to_all | solution.py:103
  242.7 10.2 %all-to-all-done.4 = bf16[64,2,384]{2,1,0:T(2,128)(2,1)S(1)} async-done(((bf16[64,2,384]{2,1,0:T(2,128)(2,1)}), bf16[64,2,384]{2,1,0:T(2,128)(2,1)S(1)}, u32[]{:S(2)}, u32[]{:S(2)}) %all-to-all-start.4) | async-done | bytes 98336 | tf_op jit(solution)/shard_map/all_to_all | solution.py:103
  252.9 1.6 scatter_custom_fusion.3
  (41 shorter events, 1.2 us)
Async XLA Ops:
  6.5 1.3 copy-start
  6.5 28.8 %reduce-scatter.4.cloned.1.call-start = ((), (), s32[]{:S(2)}) async-start(), calls=%async_computation.8 | async-start | bytes 491520
  9.1 1.8 copy-start.4
  9.1 2.0 copy-start.6
  9.1 2.2 copy-start.3
  10.1 26.3 %copy-start.1 = (bf16[128,384]{1,0:T(8,128)(2,1)S(1)}, bf16[128,384]{1,0:T(8,128)(2,1)}, u32[]{:S(2)}) copy-start(bf16[128,384]{1,0:T(8,128)(2,1)} %param.12) | copy-start | bytes 294916
  10.1 99.2 %all-gather.5.cloned.1.call-start = ((), (), s32[]{:S(2)}) async-start(), calls=%async_computation.6 | async-start | bytes 5898240 | tf_op jit(solution)/shard_map/all_gather | solution.py:34
  11.7 35.1 %copy-start.2 = (f32[1536]{0:T(1024)S(1)}, f32[1536]{0:T(1024)}, u32[]{:S(2)}) copy-start(f32[1536]{0:T(1024)} %param.13) | copy-start | bytes 18436
  53.8 55.5 %all-to-all-start.1 = ((bf16[64,1,8,1536]{3,2,1,0:T(8,128)(2,1)}), bf16[64,1,8,1536]{3,2,1,0:T(8,128)(2,1)S(1)}, u32[]{:S(2)}, u32[]{:S(2)}) async-start(bf16[64,1,8,1536]{3,2,1,0:T(8,128)(2,1)} %bitcast.7), calls=%async_computation.1 | async-start | bytes 3145728 | tf_op jit(solution)/shard_map/all_to_all | solution.py:74
  69.6 62.6 %all-gather.7.cloned.1.call-start = ((), (), s32[]{:S(2)}) async-start(), calls=%async_computation.7 | async-start | bytes 2949120 | tf_op jit(solution)/shard_map/all_gather | solution.py:35
  142.7 23.7 %all-to-all-start.2 = ((bf16[64,1,8,4,384]{4,2,0,1,3:T(8,128)(2,1)}), bf16[64,1,8,4,384]{4,2,0,1,3:T(8,128)(2,1)S(1)}, u32[]{:S(2)}, u32[]{:S(2)}) async-start(bf16[64,1,8,4,384]{4,2,0,1,3:T(8,128)(2,1)} %copy.39), calls=%async_computation.2 | async-start | bytes 3145728 | tf_op jit(solution)/shard_map/all_to_all | solution.py:85
  166.4 20.9 %all-to-all-start = ((s32[64,1,2]{2,1,0:T(1,128)}), s32[64,1,2]{2,1,0:T(1,128)S(1)}, u32[]{:S(2)}, u32[]{:S(2)}) async-start(s32[64,1,2]{2,1,0:T(1,128)} %bitcast), calls=%async_computation | async-start | bytes 65536 | tf_op jit(solution)/shard_map/all_to_all | solution.py:110
  187.3 4.9 %copy-start.5 = (f32[128,4]{0,1:T(4,128)S(1)}, f32[128,4]{0,1:T(4,128)}, u32[]{:S(2)}) copy-start(f32[128,4]{0,1:T(4,128)} %param.15) | copy-start | bytes 6148
  187.3 44.7 %all-to-all-start.3 = ((bf16[64,1,32,384]{3,2,1,0:T(8,128)(2,1)}), bf16[64,1,32,384]{3,2,1,0:T(8,128)(2,1)S(1)}, u32[]{:S(2)}, u32[]{:S(2)}) async-start(bf16[64,1,32,384]{3,2,1,0:T(8,128)(2,1)} %bitcast.68), calls=%async_computation.3 | async-start | bytes 3145728 | tf_op jit(solution)/shard_map/all_to_all | solution.py:87
  236.5 16.3 %all-to-all-start.4 = ((bf16[64,2,384]{2,1,0:T(2,128)(2,1)}), bf16[64,2,384]{2,1,0:T(2,128)(2,1)S(1)}, u32[]{:S(2)}, u32[]{:S(2)}) async-start(bf16[64,2,384]{2,1,0:T(2,128)(2,1)} %reshape.349), calls=%async_computation.4 | async-start | bytes 196608 | tf_op jit(solution)/shard_map/all_to_all | solution.py:103
Sparse Core Ops, SparseCore 0:
  10.2 25.1 reduce-scatter.3
  37.2 57.0 all-gather.4
  96.1 36.0 all-gather.6

commit v3 on v2

--- a/solution.py
+++ b/solution.py
@@ -31,8 +31,15 @@
     me_narrow = lax.axis_index("narrow")
 
     slot_local = w_in.shape[0]
-    w_in_all = lax.all_gather(w_in, "narrow", axis=0, tiled=False)
-    w_down_all = lax.all_gather(w_down, "narrow", axis=0, tiled=False)
+    hid_local = w_down.shape[1]
+    both = jnp.concatenate(
+        [w_in.reshape(slot_local, 2 * hid_local, model_width), w_down], axis=1
+    )
+    both = lax.all_gather(both, "narrow", axis=0, tiled=False)
+    w_in_all = both[:, :, : 2 * hid_local].reshape(
+        narrow_count, slot_local, 2, hid_local, model_width
+    )
+    w_down_all = both[:, :, 2 * hid_local :]
 
     partial_terms = jnp.dot(attn_heads, w_out, preferred_element_type=jnp.float32)
     projected = lax.psum_scatter(
@@ -99,18 +106,17 @@
     packed_index = target_dev * pair_rows + running_rank(choose_target)
     packed = jnp.zeros((row_count, width_local), jnp.bfloat16).at[packed_index].set(mixed)
     places = jnp.zeros((row_count,), jnp.int32).at[packed_index].set(target_place)
-    arrived_rows, arrived_places = (
-        lax.all_to_all(
-            packed.reshape(wide_count, pair_rows, width_local),
-            "wide",
-            split_axis=0,
-            concat_axis=0,
-            tiled=True,
-        ),
-        lax.all_to_all(
-            places.reshape(wide_count, pair_rows), "wide", split_axis=0, concat_axis=0, tiled=True
-        ),
+    assert row_count <= 256 and pair_rows <= width_local
+    place_row = jnp.zeros((wide_count, 1, width_local), jnp.bfloat16)
+    place_row = place_row.at[:, 0, :pair_rows].set(
+        places.reshape(wide_count, pair_rows).astype(jnp.bfloat16)
     )
+    packed = jnp.concatenate(
+        [packed.reshape(wide_count, pair_rows, width_local), place_row], axis=1
+    )
+    arrived_all = lax.all_to_all(packed, "wide", split_axis=0, concat_axis=0, tiled=True)
+    arrived_rows = arrived_all[:, :pair_rows]
+    arrived_places = arrived_all[:, pair_rows, :pair_rows].astype(jnp.int32)
     return (
         jnp.zeros((row_count, width_local), jnp.bfloat16)
         .at[arrived_places.reshape(-1)]

time: 262 us -> 240 us (0.916)
  waiting for transfers between devices: 151 us -> 102 us
  blocking collectives: 10.2 us -> 50 us
  starting transfers between devices: 42.3 us -> 27.8 us
  matrix products: 15.1 us -> 11.6 us
  local copies, waits for them, and re-layouts: 23.4 us -> 26.9 us
    all_to_all x0 -> x2, blocking collectives: none -> 39.8 us  [the longest x1 23 us: local(): lax.all_to_all(summed, 'narrow', split_axis=3, concat_axis=2, tiled=True)]
    all_to_all x1, waiting for transfers between devices: 39 us -> 0.01 us  [local(): lax.all_to_all(outgoing, 'wide', split_axis=0, concat_axis=0, tiled=True)]
    all_to_all x3 -> x0, waiting for transfers between devices: 35.8 us -> none  [the longest x1 17.7 us: local(): lax.all_to_all(summed, 'narrow', split_axis=3, concat_axis=2, tiled=True)]
    all_gather x2 -> x1, waiting for transfers between devices: 15.3 us -> 44.3 us  [local(): both = lax.all_gather(both, 'narrow', axis=0, tiled=False)]
    all_to_all x3 -> x0, starting transfers between devices: 21.6 us -> none  [the longest x1 11.7 us: local(): lax.all_to_all(places.reshape(wide_count, pair_rows), 'wide', split_axis=...]
    all_to_all x1, starting transfers between devices: 4.91 us -> 12.1 us  [local(): lax.all_to_all(summed, 'wide', split_axis=0, concat_axis=0, tiled=True)]
    slice x1 -> x2, local copies, waits for them, and re-layouts: 0.23 us -> 4.93 us  [the longest x1 4.86 us: local(): both[:, :, :2 * hid_local]]
    unnamed x4 -> x3, waiting for transfers between devices: 22.3 us -> 19.5 us
  transfers between devices with their start and end apart: 8 -> 4, of which waited for: 7 -> 3; matrix products, arithmetic and copies ran while one was open for 9% -> 8% of each run, Pallas kernels for 0% -> 0%
where the time goes in v3:
time: 240 us; the launch traced here: 239 us
  waiting for transfers between devices  102 us (42%)
  blocking collectives  50 us (21%)
  starting transfers between devices  27.8 us (12%)
  local copies, waits for them, and re-layouts  26.9 us (11%)
  between operations  13.7 us (6%)
  matrix products  11.6 us (5%)
  other arithmetic  7.02 us (3%)
    all_gather x1, waiting for transfers between devices, local(): both = lax.all_gather(both, 'narrow', axis=0, tiled=False)  44.3 us
    all_to_all x1, waiting for transfers between devices, local(): lax.all_to_all(summed, 'wide', split_axis=0, concat_axis=0, tiled=True)  38 us
    all_to_all x1, blocking collectives, local(): lax.all_to_all(summed, 'narrow', split_axis=3, concat_axis=2, tiled=True)  23 us
    unnamed x3, waiting for transfers between devices  19.5 us
    all_to_all x1, blocking collectives, local(): lax.all_to_all(packed, 'wide', split_axis=0, concat_axis=0, tiled=True)  16.8 us
    all_to_all x1, starting transfers between devices, local(): lax.all_to_all(outgoing, 'wide', split_axis=0, concat_axis=0, tiled=True)  15.6 us
    all_to_all x1, starting transfers between devices, local(): lax.all_to_all(summed, 'wide', split_axis=0, concat_axis=0, tiled=True)  12.1 us
    all_gather x1, blocking collectives, local(): lax.all_gather(hidden, 'narrow', axis=1, tiled=True).astype(jnp.float32)  10.2 us
  transfers between devices with their start and end apart: 4, of which 3 were waited for; matrix products, arithmetic and copies ran while one was open for 8% of the time, Pallas kernels for 0%

profile of v3, /device:TPU:1, one launch (start us, length us, event | category | flops | bytes accessed | tf_op | source)
XLA Modules:
  0.0 238.9 jit_solution(3613635565145867335)
XLA Ops:
  6.5 1.3 copy-done
  7.8 1.3 convolution_convert_fusion
  9.1 1.0 copy.54
  10.1 1.4 pad_maximum_fusion
  11.6 0.6 copy-done.6
  12.2 0.1 copy.39
  12.3 0.1 eq.94
  12.5 0.1 reshape.377
  12.7 0.2 reduce_window_sum.38
  12.9 0.1 fusion.22
  13.1 0.9 multiply_reduce_fusion.1
  14.1 0.1 add_select_fusion
  14.2 1.2 reduce-window.6
  15.4 0.2 slice_reduce_fusion
  15.7 0.1 fusion.13
  15.9 19.5 %reduce-scatter.4.cloned.1.call-done = bf16[384,128]{1,0:T(8,128)(2,1)} async-done(((bf16[1536,128]{1,0:T(8,128)(2,1)}), bf16[384,128]{1,0:T(8,128)(2,1)}) %reduce-scatter.4.cloned.1.call-update) | async-done | bytes 98320
  35.4 1.0 copy.55
  36.4 10.2 %all_gather.11 = bf16[128,1536]{1,0:T(8,128)(2,1)S(1)} all-gather(bf16[128,384]{1,0:T(8,128)(2,1)S(1)} %add_convert_fusion.1), channel_id=1, replica_groups=mesh['wide'=64,'narrow'=4] {'narrow'}, dimensions={1}, use_global_device_ids=true | all-gather | bytes 491520 | tf_op jit(solution)/shard_map/all_gather | solution.py:50
  46.6 0.2 fusion.6
  46.8 0.2 fusion.8
  47.0 0.4 broadcast_in_dim.24
  47.4 1.4 reshape.402
  48.8 5.2 %scatter_custom_fusion = bf16[512,1536]{1,0:T(8,128)(2,1)} fusion(s32[512]{0:T(512)S(1)} %bitcast.85, bf16[512,1536]{1,0:T(8,128)(2,1)} %reshape.402, bf16[]{:T(256)} %constant.111.clone.1), kind=kCustom, calls=%fused_computation.26 | custom fusion | bytes 1573376 | tf_op jit(solution)/shard_map/scatter | solution.py:78
  54.0 15.6 %all-to-all-start = ((bf16[64,1,8,1536]{3,2,1,0:T(8,128)(2,1)}), bf16[64,1,8,1536]{3,2,1,0:T(8,128)(2,1)S(1)}, u32[]{:S(2)}, u32[]{:S(2)}) async-start(bf16[64,1,8,1536]{3,2,1,0:T(8,128)(2,1)} %bitcast.14), calls=%async_computation | async-start | bytes 3145728 | tf_op jit(solution)/shard_map/all_to_all | solution.py:81
  69.6 44.3 %all-gather.3.cloned.1.call-done = bf16[4,576,1536]{2,1,0:T(8,128)(2,1)} async-done(((bf16[1,576,1536]{2,1,0:T(8,128)(2,1)}), bf16[4,576,1536]{2,1,0:T(8,128)(2,1)}) %all-gather.3.cloned.1.call-update) | async-done | bytes 7077904 | tf_op jit(solution)/shard_map/all_gather | solution.py:38
  114.0 4.9 %slice.58 = bf16[4,1,384,1536]{3,2,0,1:T(8,128)(2,1)} slice(bf16[4,1,576,1536]{3,2,0,1:T(8,128)(2,1)} %bitcast.75), slice={[0:4], [0:1], [0:384], [0:1536]} | slice | bytes 9437184 | tf_op jit(solution)/shard_map/slice | solution.py:39
  118.8 5.3 %convolution_bitcast_fusion = f32[64,1,8,2,4,192]{5,0,2,3,4,1:T(8,128)S(1)} fusion(bf16[4,2,192,1536,1]{3,2,4,1,0:T(8,128)(2,1)} %bitcast.74, bf16[64,1,8,1536]{3,2,1,0:T(8,128)(2,1)S(1)} %all-to-all-done), kind=kOutput, calls=%fused_computation.10 | convolution fusion | flops 2415919104 | bytes 9437184 | tf_op jit(solution)/shard_map/nscd,qsghd->nscgqh/dot_general | solution.py:82
  124.1 5.0 %convert_reduce_fusion = bf16[1536,64,8]{0,1,2:T(8,128)(2,1)} fusion(bf16[4,1,576,1536]{3,2,0,1:T(8,128)(2,1)} %bitcast.76, f32[64,1,8,2,4,192]{5,0,2,3,4,1:T(8,128)S(1)} %convolution_bitcast_fusion), kind=kOutput, calls=%fused_computation.5 | convolution fusion | flops 1214644224 | bytes 7077888 | tf_op jit(solution)/shard_map/nscqh,qshd->qnscd/dot_general | solution.py:86
  129.2 3.0 %reshape.436 = bf16[64,1,8,4,384]{4,3,0,2,1:T(4,128)(2,1)S(1)} reshape(bf16[64,8,1536]{2,0,1:T(8,128)(2,1)} %bitcast.77) | data formatting | bytes 3145728 | tf_op jit(solution)/shard_map/reshape | solution.py:91
  132.1 0.9 copy.45
  133.1 23.0 %all_to_all.30 = bf16[64,1,8,4,384]{4,2,0,1,3:T(8,128)(2,1)S(1)} all-to-all(bf16[64,1,8,4,384]{4,2,0,1,3:T(8,128)(2,1)S(1)} %copy.45), channel_id=1, replica_groups=mesh['wide'=64,'narrow'=4] {'narrow'}, dimensions={3} | all-to-all | bytes 3145728 | tf_op jit(solution)/shard_map/all_to_all | solution.py:92
  156.0 1.3 copy.66
  157.3 12.1 %all-to-all-start.2 = ((bf16[64,1,32,384]{3,2,1,0:T(8,128)(2,1)}), bf16[64,1,32,384]{3,2,1,0:T(8,128)(2,1)S(1)}, u32[]{:S(2)}, u32[]{:S(2)}) async-start(bf16[64,1,32,384]{3,2,1,0:T(8,128)(2,1)} %bitcast.73), calls=%async_computation.2 | async-start | bytes 3145728 | tf_op jit(solution)/shard_map/all_to_all | solution.py:94
  169.4 0.1 copy.38
  169.7 0.2 reduce_window_sum.37
  169.8 0.2 select_reduce_fusion.1
  170.0 1.0 scatter_custom_fusion.2
  171.0 0.2 convert_element_type.118
  171.2 38.0 %all-to-all-done.2 = bf16[64,1,32,384]{3,2,1,0:T(8,128)(2,1)S(1)} async-done(((bf16[64,1,32,384]{3,2,1,0:T(8,128)(2,1)}), bf16[64,1,32,384]{3,2,1,0:T(8,128)(2,1)S(1)}, u32[]{:S(2)}, u32[]{:S(2)}) %all-to-all-start.2) | async-done | bytes 1572896 | tf_op jit(solution)/shard_map/all_to_all | solution.py:94
  209.2 1.9 gather_fusion
  211.1 0.2 reshape.388
  211.3 0.5 multiply_reduce_fusion.2
  211.9 1.1 scatter_custom_fusion.1
  213.0 0.2 fusion.12
  213.2 16.8 %all_to_all.31 = bf16[64,3,384]{2,1,0:T(4,128)(2,1)S(1)} all-to-all(bf16[64,3,384]{2,1,0:T(4,128)(2,1)S(1)} %fusion.12), channel_id=1, replica_groups=mesh['wide'=64,'narrow'=4] {'wide'}, dimensions={0} | all-to-all | bytes 294912 | tf_op jit(solution)/shard_map/all_to_all | solution.py:117
  230.1 0.1 fusion.20
  230.2 0.1 reshape.389
  230.4 1.6 scatter_custom_fusion.3
  (42 shorter events, 0.7 us)
Async XLA Ops:
  6.5 1.3 copy-start
  6.5 3.6 %copy-start.1 = (bf16[1,2,192,1536]{3,2,1,0:T(8,128)(2,1)S(1)}, bf16[1,2,192,1536]{3,2,1,0:T(8,128)(2,1)}, u32[]{:S(2)}) copy-start(bf16[1,2,192,1536]{3,2,1,0:T(8,128)(2,1)} %param.20) | copy-start | bytes 3538948
  6.5 3.6 %copy-start.2 = (bf16[1,192,1536]{2,1,0:T(8,128)(2,1)S(1)}, bf16[1,192,1536]{2,1,0:T(8,128)(2,1)}, u32[]{:S(2)}) copy-start(bf16[1,192,1536]{2,1,0:T(8,128)(2,1)} %param.21) | copy-start | bytes 1769476
  6.5 28.8 %reduce-scatter.4.cloned.1.call-start = ((), (), s32[]{:S(2)}) async-start(), calls=%async_computation.6 | async-start | bytes 491520
  10.1 103.9 %all-gather.3.cloned.1.call-start = ((), (), s32[]{:S(2)}) async-start(), calls=%async_computation.5 | async-start | bytes 8847360 | tf_op jit(solution)/shard_map/all_gather | solution.py:38
  11.6 0.7 copy-start.6
  11.6 0.9 copy-start.8
  11.6 1.1 copy-start.5
  11.6 24.8 %copy-start.3 = (bf16[128,384]{1,0:T(8,128)(2,1)S(1)}, bf16[128,384]{1,0:T(8,128)(2,1)}, u32[]{:S(2)}) copy-start(bf16[128,384]{1,0:T(8,128)(2,1)} %param.14) | copy-start | bytes 294916
  12.2 34.6 %copy-start.4 = (f32[1536]{0:T(1024)S(1)}, f32[1536]{0:T(1024)}, u32[]{:S(2)}) copy-start(f32[1536]{0:T(1024)} %param.15) | copy-start | bytes 18436
  54.0 64.9 %all-to-all-start = ((bf16[64,1,8,1536]{3,2,1,0:T(8,128)(2,1)}), bf16[64,1,8,1536]{3,2,1,0:T(8,128)(2,1)S(1)}, u32[]{:S(2)}, u32[]{:S(2)}) async-start(bf16[64,1,8,1536]{3,2,1,0:T(8,128)(2,1)} %bitcast.14), calls=%async_computation | async-start | bytes 3145728 | tf_op jit(solution)/shard_map/all_to_all | solution.py:81
  157.3 12.1 %copy-start.7 = (f32[128,4]{0,1:T(4,128)S(1)}, f32[128,4]{0,1:T(4,128)}, u32[]{:S(2)}) copy-start(f32[128,4]{0,1:T(4,128)} %param.17) | copy-start | bytes 6148
  157.3 51.8 %all-to-all-start.2 = ((bf16[64,1,32,384]{3,2,1,0:T(8,128)(2,1)}), bf16[64,1,32,384]{3,2,1,0:T(8,128)(2,1)S(1)}, u32[]{:S(2)}, u32[]{:S(2)}) async-start(bf16[64,1,32,384]{3,2,1,0:T(8,128)(2,1)} %bitcast.73), calls=%async_computation.2 | async-start | bytes 3145728 | tf_op jit(solution)/shard_map/all_to_all | solution.py:94
Sparse Core Ops, SparseCore 0:
  10.2 25.1 reduce-scatter.3
  37.2 76.7 all-gather.2
